TPU v7x, 512 devices: a whole 4x4x16 slice. The times are simulated.
512 devices in a mesh: kv: 8 (over y, core), pages: 64 (over x, z).
Axes of the slice: x: 4, y: 4, z: 16, core: 2. Of those that a mesh axis runs over, the one named last changes fastest.
Arguments:
- tokens: int32 [2, 64], replicated, may hold values from 0 to 31999
- prompt_len: int32 [8], replicated, may hold values from 193 to 8192, as said below
- page_table: int32 [8, 64], replicated, may hold values from -1 to 511, as said below
- parents: int32 [2, 64], replicated, may hold values from 0 to 63, as said below
- embedding: bfloat16 [32000, 7168], P('kv', 'pages'), may hold values from -6 to 6
- norm_gain: bfloat16 [7168], P('pages'), may hold values from 0.099609375 to 1.8984375
- w_qkv: bfloat16 [7168, 9216], P('pages', 'kv'), may hold values from -0.0625 to 0.0625
- w_out: bfloat16 [7168, 7168], P('kv', 'pages'), may hold values from -0.8984375 to 0.8984375
- history: bfloat16 [2, 64, 13, 1024], P(None, None, None, 'kv'), may hold values from -6 to 6
- kv_pool: bfloat16 [2, 512, 128, 1024], P(None, 'pages', None, 'kv'), may hold values from -400 to 400
Outputs:
- hidden: bfloat16 [2, 64, 7168], P(None, None, 'pages')
- history_out: bfloat16 [2, 64, 15, 1024], P(None, None, None, 'kv')
Inputs may be any that keep to these rules, and one draw needn't show every extreme that they name: `prompt_len`: each prompt is either long, within 512 tokens below 8192, or short, within 64 tokens below 256; some group's prompt has exactly 8192 tokens. For j below prompt_len[g] / 128 rounded up, page_table[g, j] is the slot holding tokens j * 128 to j * 128 + 127 of group g's prompt; no slot is named twice; all other entries are -1. parents[t, b] is a beam of b's group; at the first step the first and the last beam of every group continue their own history.
All inputs are finite; a program needn't handle non-finite values.
Results may differ from a plain program's by a relative error of at most 0.015.
The roundings to bfloat16 on the way count: a program that leaves them out, or rounds other values in their place, can miss the bound.
Values may be sent and summed in bfloat16 or wider, within the bound.
No kernel may reach another device: no remote copies, remote signals or barrier semaphores. Data moves between devices by JAX's collectives and lax.ppermute only.
A program may use at most 128 MiB of HBM per device.

v0:
```python
import jax
import jax.numpy as jnp
from jax import lax
from jax.sharding import PartitionSpec as P

D = 7168
KV_HEADS = 8
HEAD_DIM = 128
GROUPS = 8
BEAMS = 8
PRIOR = 13
PAGE = 128
PER_KV = 7
HISTORY = 15
MAX_PAGES = 64
THETA = 5000000.0
EPSILON = 1e-05
NEGATIVE = -1e30


def rotate(values, positions):
    half_dim = HEAD_DIM // 2
    frequency = THETA ** (-(2.0 * jnp.arange(half_dim, dtype=jnp.float32)) / HEAD_DIM)
    angles = positions.astype(jnp.float32)[:, None] * frequency[None, :]
    cosine = jnp.cos(angles)[:, None, None, :]
    sine_part = jnp.sin(angles)[:, None, None, :]
    lower_part = values[..., :half_dim]
    upper_part = values[..., half_dim:]
    return jnp.concatenate(
        [
            lower_part * cosine - upper_part * sine_part,
            upper_part * cosine + lower_part * sine_part,
        ],
        axis=-1,
    )


def finish_rows(summed, norm_sums, row_ids, prompt_len, num_seqs, local_heads):
    inverse_rms = lax.rsqrt(norm_sums / D + EPSILON)
    projected = (summed * inverse_rms[:, None]).reshape(-1, local_heads, PER_KV + 2, HEAD_DIM)
    positions = jnp.take(prompt_len, row_ids % num_seqs // BEAMS) + PRIOR + row_ids // num_seqs
    turned = rotate(projected[:, :, : PER_KV + 1], positions)
    return jnp.concatenate([turned, projected[:, :, PER_KV + 1 :]], axis=2).astype(jnp.bfloat16)


def combine(earlier, later):
    peak = jnp.maximum(earlier[0], later[0])
    weight_one = jnp.exp(earlier[0] - peak)
    weight_two = jnp.exp(later[0] - peak)
    return (
        peak,
        earlier[1] * weight_one + later[1] * weight_two,
        earlier[2] * weight_one[:, None] + later[2] * weight_two[:, None],
    )


def reduce_rows(packed, axis):
    sources = lax.axis_size(axis)
    split = packed.reshape(sources, packed.shape[0] // sources, *packed.shape[1:])
    return jnp.sum(lax.all_to_all(split, axis, 0, 0, tiled=False), axis=0)


def per_device(
    tokens, prompt_len, page_table, parents, embedding, norm_gain, w_qkv, w_out, history, kv_pool
):
    num_steps, num_seqs = tokens.shape
    row_count = num_steps * num_seqs
    page_devices = lax.axis_size("pages")
    page_index = lax.axis_index("pages")
    local_heads = KV_HEADS // lax.axis_size("kv")
    kv_width = local_heads * HEAD_DIM
    inv_root = 1.0 / jnp.sqrt(jnp.float32(HEAD_DIM))
    vocab_local = embedding.shape[0]
    local_ids = tokens.reshape(-1) - lax.axis_index("kv") * vocab_local
    inside = (local_ids >= 0) & (local_ids < vocab_local)
    picked = jnp.take(embedding, jnp.clip(local_ids, 0, vocab_local - 1), axis=0)
    found = jnp.where(inside[:, None], picked, jnp.zeros_like(picked))
    embedded = lax.psum(found, "kv")
    widened = embedded.astype(jnp.float32)
    squares = jnp.sum(widened * widened, axis=1)
    normed = (widened * norm_gain.astype(jnp.float32)).astype(jnp.bfloat16)
    partial_value = jnp.dot(normed, w_qkv, preferred_element_type=jnp.float32)
    qkv_cols = partial_value.shape[1]
    packed = jnp.concatenate(
        [partial_value, squares[:, None], jnp.zeros((row_count, 127), jnp.float32)], axis=1
    )
    reduced = reduce_rows(packed, "pages")
    rows_per = row_count // page_devices
    my_rows = page_index * rows_per + jnp.arange(rows_per, dtype=jnp.int32)
    mine = finish_rows(
        reduced[:, :qkv_cols], reduced[:, qkv_cols], my_rows, prompt_len, num_seqs, local_heads
    )
    projected = lax.all_gather(
        mine.reshape(rows_per, qkv_cols), "pages", axis=0, tiled=True
    ).reshape(row_count, local_heads, PER_KV + 2, HEAD_DIM)
    queries = projected[:, :, :PER_KV]
    fresh_kv = jnp.stack([projected[:, :, PER_KV], projected[:, :, PER_KV + 1]]).reshape(
        2, num_steps, num_seqs, kv_width
    )
    buffer = jnp.concatenate(
        [history, jnp.zeros((2, num_seqs, num_steps, kv_width), jnp.bfloat16)], axis=2
    )
    snapshots = []
    for step_index in range(num_steps):
        buffer = jnp.take(buffer, parents[step_index], axis=1)
        buffer = buffer.at[:, :, PRIOR + step_index].set(fresh_kv[:, step_index])
        snapshots.append(buffer)
    stacked = jnp.stack(snapshots)
    tail_keys = stacked[:, 0].reshape(num_steps, num_seqs, HISTORY, local_heads, HEAD_DIM)
    tail_vals = stacked[:, 1].reshape(num_steps, num_seqs, HISTORY, local_heads, HEAD_DIM)
    step_query = queries.reshape(num_steps, num_seqs, local_heads, PER_KV, HEAD_DIM)
    tail_len = PRIOR + 1 + jnp.arange(num_steps, dtype=jnp.int32)
    tail_valid = (jnp.arange(HISTORY, dtype=jnp.int32)[None, :] < tail_len[:, None])[
        :, None, None, None, :
    ]
    tail_scores = (
        jnp.einsum("tbkhd,tblkd->tbkhl", step_query, tail_keys, preferred_element_type=jnp.float32)
        * inv_root
    )
    tail_scores = jnp.where(tail_valid, tail_scores, NEGATIVE)
    tail_peak = jnp.max(tail_scores, axis=-1)
    tail_exp = jnp.where(tail_valid, jnp.exp(tail_scores - tail_peak[..., None]), 0.0)
    tail_total = jnp.sum(tail_exp, axis=-1)
    tail_acc = jnp.einsum(
        "tbkhl,tblkd->tbkhd",
        tail_exp.astype(jnp.bfloat16),
        tail_vals,
        preferred_element_type=jnp.float32,
    )
    tail_part = (tail_peak.reshape(-1), tail_total.reshape(-1), tail_acc.reshape(-1, HEAD_DIM))
    slot_rows = kv_pool.shape[1]
    slot_ids = page_index * slot_rows + jnp.arange(slot_rows, dtype=jnp.int32)
    matches = page_table[:, :, None] == slot_ids[None, None, :]
    slot_used = jnp.any(matches, axis=(0, 1))
    owner_group = jnp.sum(
        jnp.where(matches, jnp.arange(GROUPS, dtype=jnp.int32)[:, None, None], 0), axis=(0, 1)
    )
    page_number = jnp.sum(
        jnp.where(matches, jnp.arange(MAX_PAGES, dtype=jnp.int32)[None, :, None], 0), axis=(0, 1)
    )
    length = jnp.take(prompt_len, owner_group)
    live_tok = slot_used[:, None] & (
        page_number[:, None] * PAGE + jnp.arange(PAGE, dtype=jnp.int32)[None, :] < length[:, None]
    )
    live_full = live_tok[None, :, None, :]
    grouped = queries.reshape(num_steps, GROUPS, BEAMS, local_heads, PER_KV, HEAD_DIM)
    chosen = jnp.take(grouped, owner_group, axis=1)
    query_rows = num_steps * BEAMS * PER_KV
    chosen = jnp.transpose(chosen, (3, 1, 0, 2, 4, 5)).reshape(
        local_heads, slot_rows, query_rows, HEAD_DIM
    )
    page_keys = jnp.transpose(
        kv_pool[0].reshape(slot_rows, PAGE, local_heads, HEAD_DIM), (2, 0, 1, 3)
    )
    page_vals = jnp.transpose(
        kv_pool[1].reshape(slot_rows, PAGE, local_heads, HEAD_DIM), (2, 0, 1, 3)
    )
    scores = (
        jnp.einsum("ksqd,kspd->ksqp", chosen, page_keys, preferred_element_type=jnp.float32)
        * inv_root
    )
    scores = jnp.where(live_full, scores, NEGATIVE)
    slot_peak = jnp.max(scores, axis=-1)
    slot_exp = jnp.where(live_full, jnp.exp(scores - slot_peak[..., None]), 0.0)
    slot_total = jnp.sum(slot_exp, axis=-1)
    slot_acc = jnp.einsum(
        "ksqp,kspd->ksqd",
        slot_exp.astype(jnp.bfloat16),
        page_vals,
        preferred_element_type=jnp.float32,
    )
    member = (owner_group[:, None] == jnp.arange(GROUPS, dtype=jnp.int32)[None, :]) & slot_used[
        :, None
    ]
    spread = jnp.where(member[None, :, :, None], slot_peak[:, :, None, :], NEGATIVE)
    group_peak = jnp.max(spread, axis=1)
    slot_base = jnp.take(group_peak, owner_group, axis=1)
    weight = jnp.where(slot_used[None, :, None], jnp.exp(slot_peak - slot_base), 0.0)
    member_f = member.astype(jnp.float32)
    group_total = jnp.einsum(
        "sg,ksq->kgq", member_f, slot_total * weight, precision=lax.Precision.HIGHEST
    )
    group_acc = jnp.einsum(
        "sg,ksqd->kgqd", member_f, slot_acc * weight[..., None], precision=lax.Precision.HIGHEST
    )
    order_small = (2, 1, 3, 0, 4)
    peak_rows = jnp.transpose(
        group_peak.reshape(local_heads, GROUPS, num_steps, BEAMS, PER_KV), order_small
    )
    total_rows = jnp.transpose(
        group_total.reshape(local_heads, GROUPS, num_steps, BEAMS, PER_KV), order_small
    )
    acc_rows = jnp.transpose(
        group_acc.reshape(local_heads, GROUPS, num_steps, BEAMS, PER_KV, HEAD_DIM),
        (2, 1, 3, 0, 4, 5),
    )
    local_part = (peak_rows.reshape(-1), total_rows.reshape(-1), acc_rows.reshape(-1, HEAD_DIM))
    with_tail = combine(local_part, tail_part)
    first = page_index == 0
    part = jax.tree.map(lambda a, b: jnp.where(first, a, b), with_tail, local_part)
    attn_rows = part[0].shape[0]
    share = attn_rows // page_devices
    stats = jnp.zeros((page_devices, 2, HEAD_DIM), jnp.float32)
    stats = stats.at[:, 0, :share].set(part[0].reshape(page_devices, share))
    stats = stats.at[:, 1, :share].set(part[1].reshape(page_devices, share))
    sent = jnp.concatenate([part[2].reshape(page_devices, share, HEAD_DIM), stats], axis=1)
    received = lax.all_to_all(sent, "pages", 0, 0, tiled=False)
    src_acc = received[:, :share]
    src_peak = received[:, share, :share]
    src_total = received[:, share + 1, :share]
    top = jnp.max(src_peak, axis=0)
    scale = jnp.exp(src_peak - top[None, :])
    total = jnp.sum(src_total * scale, axis=0)
    acc = jnp.sum(src_acc * scale[:, :, None], axis=0)
    attended_mine = (acc / total[:, None]).astype(jnp.bfloat16)
    attended = lax.all_gather(attended_mine, "pages", axis=0, tiled=True)
    flat_heads = attended.reshape(row_count, local_heads * PER_KV * HEAD_DIM)
    head_terms = jnp.dot(flat_heads, w_out, preferred_element_type=jnp.float32)
    mixed_out = lax.psum(head_terms, "kv") + widened
    return (mixed_out.astype(jnp.bfloat16).reshape(num_steps, num_seqs, -1), buffer)


def solution(mesh):
    placed = (
        P(),
        P(),
        P(),
        P(),
        P("kv", "pages"),
        P("pages"),
        P("pages", "kv"),
        P("kv", "pages"),
        P(None, None, None, "kv"),
        P(None, "pages", None, "kv"),
    )
    return jax.shard_map(
        per_device,
        mesh=mesh,
        in_specs=placed,
        out_specs=(P(None, None, "pages"), P(None, None, None, "kv")),
        check_vma=False,
    )
```

profile of v0, /device:TPU:2, one launch (start us, length us, event | category | flops | bytes accessed | tf_op | source)
XLA Modules:
  0.0 330.2 jit_solution(9333004491464431049)
XLA Ops:
  0.7 0.7 copy-done.6
  2.2 1.9 copy.207
  4.2 0.7 gather_fusion.1
  5.0 25.9 %psum.14 = bf16[128,112]{0,1:T(8,128)(2,1)S(1)} all-reduce(bf16[128,112]{0,1:T(8,128)(2,1)S(1)} %select_select_fusion), channel_id=1, replica_groups=mesh['kv'=8,'pages'=64] {'kv'}, use_global_device_ids=true, to_apply=%region_3.4 | all-reduce | flops 14336 | bytes 57344 | tf_op jit(solution)/shard_map/psum | solution.py:78
  31.9 2.2 concatenate.36
  34.1 18.8 %all-to-all-start = ((f32[64,2,1280]{2,1,0:T(2,128)}), f32[64,2,1280]{2,1,0:T(2,128)S(1)}, u32[]{:S(2)}, u32[]{:S(2)}) async-start(f32[64,2,1280]{2,1,0:T(2,128)} %concatenate.36), calls=%async_computation | async-start | bytes 1310720 | tf_op jit(solution)/shard_map/all_to_all | solution.py:60
  52.9 0.7 copy-done.5
  54.1 0.6 gather_fusion
  54.8 0.6 gather_fusion.2
  56.6 1.6 gather_fusion.5
  58.6 28.0 %all-to-all-done = f32[64,2,1280]{2,1,0:T(2,128)S(1)} async-done(((f32[64,2,1280]{2,1,0:T(2,128)}), f32[64,2,1280]{2,1,0:T(2,128)S(1)}, u32[]{:S(2)}, u32[]{:S(2)}) %all-to-all-start) | async-done | bytes 655392 | tf_op jit(solution)/shard_map/all_to_all | solution.py:60
  87.2 94.1 %all-gather = bf16[64,2,1152]{2,1,0:T(2,128)(2,1)S(1)} all-gather(bf16[1,2,1152]{2,1,0:T(2,128)(2,1)S(1)} %reshape.977), channel_id=1, replica_groups=mesh['kv'=8,'pages'=64] {'pages'}, dimensions={0}, use_global_device_ids=true | all-gather | bytes 299520 | tf_op jit(solution)/shard_map/all_gather | solution.py:93
  181.7 0.6 gather_fusion.3
  182.5 0.9 copy-done.4
  184.7 1.4 scatter.14
  186.6 1.6 gather_fusion.6
  192.6 0.9 pad_maximum_fusion.1
  193.5 8.4 %all-to-all-start.1 = ((f32[64,16,128]{2,1,0:T(8,128)}), f32[64,16,128]{2,1,0:T(8,128)S(1)}, u32[]{:S(2)}, u32[]{:S(2)}) async-start(f32[64,16,128]{2,1,0:T(8,128)} %pad_maximum_fusion.1), calls=%async_computation.1 | async-start | bytes 1048576 | tf_op jit(solution)/shard_map/all_to_all | solution.py:207
  201.9 0.9 copy.237
  202.8 20.7 %all-to-all-done.1 = f32[64,16,128]{2,1,0:T(8,128)S(1)} async-done(((f32[64,16,128]{2,1,0:T(8,128)}), f32[64,16,128]{2,1,0:T(8,128)S(1)}, u32[]{:S(2)}, u32[]{:S(2)}) %all-to-all-start.1) | async-done | bytes 524320 | tf_op jit(solution)/shard_map/all_to_all | solution.py:207
  223.9 80.4 %all-gather.1 = bf16[64,14,128]{2,1,0:T(8,128)(2,1)S(1)} all-gather(bf16[1,14,128]{2,1,0:T(8,128)(2,1)S(1)} %fusion.46), channel_id=1, replica_groups=mesh['kv'=8,'pages'=64] {'pages'}, dimensions={0}, use_global_device_ids=true | all-gather | bytes 232960 | tf_op jit(solution)/shard_map/all_gather | solution.py:216
  304.6 0.7 copy-done.3
  305.5 24.0 %psum.15 = f32[128,112]{0,1:T(8,128)S(1)} all-reduce(f32[128,112]{0,1:T(8,128)S(1)} %fusion.67), channel_id=1, replica_groups=mesh['kv'=8,'pages'=64] {'kv'}, use_global_device_ids=true, to_apply=%region_14.16 | all-reduce | flops 14336 | bytes 114688 | tf_op jit(solution)/shard_map/psum | solution.py:219
  329.5 0.7 copy.236
  (114 shorter events, 12.2 us)
Async XLA Ops:
  0.6 30.6 %copy-start = (bf16[112,1152]{1,0:T(8,128)(2,1)S(1)}, bf16[112,1152]{1,0:T(8,128)(2,1)}, u32[]{:S(2)}) copy-start(bf16[112,1152]{1,0:T(8,128)(2,1)} %param.26) | copy-start | bytes 774148
  0.7 0.7 copy-start.6
  1.5 0.7 copy-start.8
  34.1 20.0 %copy-start.1 = (s32[8]{0:T(128)S(1)}, s32[8]{0:T(128)}, u32[]{:S(2)}) copy-start(s32[8]{0:T(128)} %param.21) | copy-start | bytes 100
  34.1 52.5 %all-to-all-start = ((f32[64,2,1280]{2,1,0:T(2,128)}), f32[64,2,1280]{2,1,0:T(2,128)S(1)}, u32[]{:S(2)}, u32[]{:S(2)}) async-start(f32[64,2,1280]{2,1,0:T(2,128)} %concatenate.36), calls=%async_computation | async-start | bytes 1310720 | tf_op jit(solution)/shard_map/all_to_all | solution.py:60
  52.9 0.7 copy-start.5
  54.1 1.3 copy-start.2
  55.9 0.7 copy-start.7
  182.3 1.0 copy-start.4
  193.5 30.1 %all-to-all-start.1 = ((f32[64,16,128]{2,1,0:T(8,128)}), f32[64,16,128]{2,1,0:T(8,128)S(1)}, u32[]{:S(2)}, u32[]{:S(2)}) async-start(f32[64,16,128]{2,1,0:T(8,128)} %pad_maximum_fusion.1), calls=%async_computation.1 | async-start | bytes 1048576 | tf_op jit(solution)/shard_map/all_to_all | solution.py:207
  304.3 0.9 copy-start.3
where the time goes:
time: 331 us; the launch traced here: 330 us
  blocking collectives  224 us (68%)
  waiting for transfers between devices  48.7 us (15%)
  starting transfers between devices  27.2 us (8%)
  local copies, waits for them, and re-layouts  21.8 us (7%)
  other arithmetic  4.29 us (1%)
    all_gather x1, blocking collectives, per_device(): lax.all_gather(mine.reshape(rows_per, qkv_cols), 'pages', axis=0, tiled=T...  94.1 us
    all_gather x1, blocking collectives, per_device(): attended = lax.all_gather(attended_mine, 'pages', axis=0, tiled=True)  80.4 us
    all_to_all x1, waiting for transfers between devices, reduce_rows(): return jnp.sum(lax.all_to_all(split, axis, 0, 0, tiled=False), axis=0)  28 us
    psum x1, blocking collectives, per_device(): embedded = lax.psum(found, 'kv')  25.9 us
    psum x1, blocking collectives, per_device(): mixed_out = lax.psum(head_terms, 'kv') + widened  24 us
    all_to_all x1, waiting for transfers between devices, per_device(): received = lax.all_to_all(sent, 'pages', 0, 0, tiled=False)  20.7 us
    all_to_all x1, starting transfers between devices, reduce_rows(): return jnp.sum(lax.all_to_all(split, axis, 0, 0, tiled=False), axis=0)  18.8 us
    all_to_all x1, starting transfers between devices, per_device(): received = lax.all_to_all(sent, 'pages', 0, 0, tiled=False)  8.39 us
  transfers between devices with their start and end apart: 2, of which 2 were waited for; matrix products, arithmetic and copies ran while one was open for 2% of the time, Pallas kernels for 0%

commit v1 on v0

--- a/solution.py
+++ b/solution.py
@@ -213,7 +213,10 @@
     total = jnp.sum(src_total * scale, axis=0)
     acc = jnp.sum(src_acc * scale[:, :, None], axis=0)
     attended_mine = (acc / total[:, None]).astype(jnp.bfloat16)
-    attended = lax.all_gather(attended_mine, "pages", axis=0, tiled=True)
+    outcome_arr = lax.all_to_all(
+        jnp.stack([attended_mine for _ in range(lax.psum(1, "pages"))], axis=0), "pages", 0, 0
+    )
+    attended = jnp.concatenate(outcome_arr, 0)
     flat_heads = attended.reshape(row_count, local_heads * PER_KV * HEAD_DIM)
     head_terms = jnp.dot(flat_heads, w_out, preferred_element_type=jnp.float32)
     mixed_out = lax.psum(head_terms, "kv") + widened

time: 331 us -> 279 us (0.84)
  the two profiles are of different devices: /device:TPU:2 before, /device:TPU:6 now
where the time goes in v1:
time: 279 us; the launch traced here: 278 us
  blocking collectives  179 us (64%)
  waiting for transfers between devices  43.6 us (16%)
  starting transfers between devices  25.9 us (9%)
  local copies, waits for them, and re-layouts  21.9 us (8%)
  other arithmetic  3.5 us (1%)
    all_gather x1, blocking collectives, per_device(): lax.all_gather(mine.reshape(rows_per, qkv_cols), 'pages', axis=0, tiled=T...  93.6 us
    all_to_all x1, blocking collectives, per_device(): received = lax.all_to_all(sent, 'pages', 0, 0, tiled=False)  34.7 us
    all_to_all x1, waiting for transfers between devices, reduce_rows(): return jnp.sum(lax.all_to_all(split, axis, 0, 0, tiled=False), axis=0)  28 us
    psum x1, blocking collectives, per_device(): embedded = lax.psum(found, 'kv')  25.9 us
    psum x1, blocking collectives, per_device(): mixed_out = lax.psum(head_terms, 'kv') + widened  25.2 us
    all_to_all x1, starting transfers between devices, reduce_rows(): return jnp.sum(lax.all_to_all(split, axis, 0, 0, tiled=False), axis=0)  18.9 us
    all_to_all x1, waiting for transfers between devices, per_device(): lax.all_to_all(jnp.stack([attended_mine for _ in range(lax.psum(1, 'pages...  15.6 us
    all_to_all x1, starting transfers between devices, per_device(): lax.all_to_all(jnp.stack([attended_mine for _ in range(lax.psum(1, 'pages...  7.02 us
  transfers between devices with their start and end apart: 2, of which 2 were waited for; matrix products, arithmetic and copies ran while one was open for 2% of the time, Pallas kernels for 0%

profile of v1, /device:TPU:6, one launch (start us, length us, event | category | flops | bytes accessed | tf_op | source)
XLA Modules:
  0.0 278.2 jit_solution(8428687050331847994)
XLA Ops:
  0.7 0.7 copy-done.6
  1.6 0.6 copy-done.8
  2.2 1.9 copy.207
  4.2 0.7 gather_fusion.1
  5.0 25.9 %psum.14 = bf16[128,112]{0,1:T(8,128)(2,1)S(1)} all-reduce(bf16[128,112]{0,1:T(8,128)(2,1)S(1)} %select_select_fusion), channel_id=1, replica_groups=mesh['kv'=8,'pages'=64] {'kv'}, use_global_device_ids=true, to_apply=%region_3.4 | all-reduce | flops 14336 | bytes 57344 | tf_op jit(solution)/shard_map/psum | solution.py:78
  31.9 2.2 concatenate.36
  34.1 18.9 %all-to-all-start = ((f32[64,2,1280]{2,1,0:T(2,128)}), f32[64,2,1280]{2,1,0:T(2,128)S(1)}, u32[]{:S(2)}, u32[]{:S(2)}) async-start(f32[64,2,1280]{2,1,0:T(2,128)} %concatenate.36), calls=%async_computation | async-start | bytes 1310720 | tf_op jit(solution)/shard_map/all_to_all | solution.py:60
  53.1 0.7 copy-done.5
  54.3 0.6 gather_fusion
  54.9 0.6 gather_fusion.2
  56.7 1.6 gather_fusion.5
  58.8 28.0 %all-to-all-done = f32[64,2,1280]{2,1,0:T(2,128)S(1)} async-done(((f32[64,2,1280]{2,1,0:T(2,128)}), f32[64,2,1280]{2,1,0:T(2,128)S(1)}, u32[]{:S(2)}, u32[]{:S(2)}) %all-to-all-start) | async-done | bytes 655392 | tf_op jit(solution)/shard_map/all_to_all | solution.py:60
  87.4 93.6 %all-gather = bf16[64,2,1152]{2,1,0:T(2,128)(2,1)S(1)} all-gather(bf16[1,2,1152]{2,1,0:T(2,128)(2,1)S(1)} %reshape.981), channel_id=1, replica_groups=mesh['kv'=8,'pages'=64] {'pages'}, dimensions={0}, use_global_device_ids=true | all-gather | bytes 299520 | tf_op jit(solution)/shard_map/all_gather | solution.py:93
  181.4 0.6 gather_fusion.3
  182.1 0.9 copy-done.4
  184.4 1.4 scatter.14
  186.3 1.6 gather_fusion.6
  192.3 34.7 %all_to_all.15 = f32[64,16,128]{2,1,0:T(8,128)S(1)} all-to-all(f32[64,16,128]{2,1,0:T(8,128)S(1)} %pad_maximum_fusion.1), channel_id=1, replica_groups=mesh['kv'=8,'pages'=64] {'pages'}, dimensions={0} | all-to-all | bytes 1048576 | tf_op jit(solution)/shard_map/all_to_all | solution.py:207
  227.5 0.7 stack.20
  228.2 7.0 %all-to-all-start.2 = ((bf16[64,14,128]{2,1,0:T(8,128)(2,1)}), bf16[64,14,128]{2,1,0:T(8,128)(2,1)S(1)}, u32[]{:S(2)}, u32[]{:S(2)}) async-start(bf16[64,14,128]{2,1,0:T(8,128)(2,1)} %stack.20), calls=%async_computation.2 | async-start | bytes 524288 | tf_op jit(solution)/shard_map/all_to_all | solution.py:216
  235.2 0.9 copy.237
  236.1 15.6 %all-to-all-done.2 = bf16[64,14,128]{2,1,0:T(8,128)(2,1)S(1)} async-done(((bf16[64,14,128]{2,1,0:T(8,128)(2,1)}), bf16[64,14,128]{2,1,0:T(8,128)(2,1)S(1)}, u32[]{:S(2)}, u32[]{:S(2)}) %all-to-all-start.2) | async-done | bytes 229408 | tf_op jit(solution)/shard_map/all_to_all | solution.py:216
  252.2 25.2 %psum.15 = f32[128,112]{0,1:T(8,128)S(1)} all-reduce(f32[128,112]{0,1:T(8,128)S(1)} %fusion.66), channel_id=1, replica_groups=mesh['kv'=8,'pages'=64] {'kv'}, use_global_device_ids=true, to_apply=%region_14.16 | all-reduce | flops 14336 | bytes 114688 | tf_op jit(solution)/shard_map/psum | solution.py:222
  277.4 0.7 copy.236
  (115 shorter events, 11.7 us)
Async XLA Ops:
  0.6 30.6 %copy-start = (bf16[112,1152]{1,0:T(8,128)(2,1)S(1)}, bf16[112,1152]{1,0:T(8,128)(2,1)}, u32[]{:S(2)}) copy-start(bf16[112,1152]{1,0:T(8,128)(2,1)} %param.26) | copy-start | bytes 774148
  0.7 0.7 copy-start.6
  1.5 0.7 copy-start.8
  34.1 20.1 %copy-start.1 = (s32[8]{0:T(128)S(1)}, s32[8]{0:T(128)}, u32[]{:S(2)}) copy-start(s32[8]{0:T(128)} %param.21) | copy-start | bytes 100
  34.1 52.6 %all-to-all-start = ((f32[64,2,1280]{2,1,0:T(2,128)}), f32[64,2,1280]{2,1,0:T(2,128)S(1)}, u32[]{:S(2)}, u32[]{:S(2)}) async-start(f32[64,2,1280]{2,1,0:T(2,128)} %concatenate.36), calls=%async_computation | async-start | bytes 1310720 | tf_op jit(solution)/shard_map/all_to_all | solution.py:60
  53.0 0.7 copy-start.5
  54.2 1.3 copy-start.2
  56.0 0.7 copy-start.7
  182.0 1.0 copy-start.4
  228.2 23.6 %all-to-all-start.2 = ((bf16[64,14,128]{2,1,0:T(8,128)(2,1)}), bf16[64,14,128]{2,1,0:T(8,128)(2,1)S(1)}, u32[]{:S(2)}, u32[]{:S(2)}) async-start(bf16[64,14,128]{2,1,0:T(8,128)(2,1)} %stack.20), calls=%async_computation.2 | async-start | bytes 524288 | tf_op jit(solution)/shard_map/all_to_all | solution.py:216
  236.1 15.9 %copy-start.3 = (bf16[896,112]{0,1:T(8,128)(2,1)S(1)}, bf16[896,112]{0,1:T(8,128)(2,1)}, u32[]{:S(2)}) copy-start(bf16[896,112]{0,1:T(8,128)(2,1)} %param.27) | copy-start | bytes 602116
